TPU v7x, 512 devices: a whole 4x8x8 slice. The times are simulated.
512 devices in a mesh: worker: 16 (over x, z_lo, core), fsdp: 32 (over z_hi, y).
Axes of the slice: x: 4, y: 8, z: 8 (z_hi: 4, z_lo: 2; z = z_hi * 2 + z_lo), core: 2. Of those that a mesh axis runs over, the one named last changes fastest.
Arguments:
- hidden: bfloat16 [9472, 65536], P('fsdp', 'worker'), may hold values from -6 to 6
- cotangent: bfloat16 [65536, 1792], P(('worker', 'fsdp')), may hold values from -6 to 6
- first_moment: bfloat16 [16, 9472, 1792], P('worker', 'fsdp'), may hold values from -0.0625 to 0.0625
- second_moment: bfloat16 [16, 9472, 1792], P('worker', 'fsdp'), may hold values from 1.21593475e-05 to 0.00024414062
- outer_momentum: bfloat16 [9472, 1792], P('fsdp', 'worker'), may hold values from -4 to 4
Outputs:
- new_momentum: float32 [9472, 1792], P('fsdp', 'worker')
All inputs are finite; a program needn't handle non-finite values.
Results may differ from a plain program's by a relative error of at most 0.0003.
Values may be sent and summed in bfloat16 or wider, within the bound.
No kernel may reach another device: no remote copies, remote signals or barrier semaphores. Data moves between devices by JAX's collectives and lax.ppermute only.
A program may use at most 64 MiB of HBM per device.

v0:
```python
import jax
import jax.numpy as jnp
from jax import lax
from jax.sharding import Mesh
from jax.sharding import PartitionSpec as P

W = ("wx", "wz", "wc")
F = ("fz", "fy")


def shards(hidden, cotangent, first_moment, second_moment, outer_momentum):
    gathered = lax.all_gather(cotangent, "fy", axis=0, tiled=True)
    gathered = lax.all_gather(gathered, "fz", axis=0, tiled=True)
    gradient = jnp.dot(hidden, gathered, preferred_element_type=jnp.float32) / gathered.shape[0]
    first_new = 0.9 * first_moment[0].astype(jnp.float32) + 0.1 * gradient
    second_new = 0.95 * second_moment[0].astype(jnp.float32) + 0.05 * gradient * gradient
    pseudo = first_new / (jnp.sqrt(second_new) + 1e-08)
    summed = lax.psum_scatter(pseudo, "wx", scatter_dimension=1, tiled=True)
    summed = lax.psum_scatter(summed, "wz", scatter_dimension=1, tiled=True)
    summed = lax.psum_scatter(summed, "wc", scatter_dimension=1, tiled=True)
    average = summed / 16
    return 0.9 * outer_momentum.astype(jnp.float32) + average


def solution(mesh):
    sizes = {"worker": (4, 2, 2), "fsdp": (4, 8)}
    fine = Mesh(mesh.devices.reshape(sizes["worker"] + sizes["fsdp"]), W + F)
    in_specs = (P(F, W), P(W + F, None), P(W, F, None), P(W, F, None), P(F, W))
    out_specs = P(F, W)
    return jax.shard_map(shards, mesh=fine, in_specs=in_specs, out_specs=out_specs, check_vma=False)
```

profile of v0, /device:TPU:1, one launch (start us, length us, event | category | flops | bytes accessed | tf_op | source)
XLA Modules:
  0.0 440.6 jit_solution(18052096988505240915)
XLA Ops:
  6.5 0.0 copy-start
  6.5 0.0 all-gather.3.cloned.1.call-start
  6.5 0.7 all-gather.3.cloned.1.call-update
  7.3 0.0 all-gather.5.cloned.1.call-start
  7.3 59.6 %all-gather.3.cloned.1.call-done = bf16[1024,1792]{1,0:T(8,128)(2,1)} async-done(((bf16[128,1792]{1,0:T(8,128)(2,1)}), bf16[1024,1792]{1,0:T(8,128)(2,1)}) %all-gather.3.cloned.1.call-update) | async-done | bytes 3670032 | tf_op jit(solution)/shard_map/all_gather | solution.py:12
  66.9 0.0 all-gather.5.cloned.1.call-update
  66.9 0.0 reduce-scatter.10.cloned.1.call-start
  67.0 263.2 %all-gather.5.cloned.1.call-done = bf16[4096,1792]{1,0:T(8,128)(2,1)} async-done(((bf16[1024,1792]{1,0:T(8,128)(2,1)}), bf16[4096,1792]{1,0:T(8,128)(2,1)}) %all-gather.5.cloned.1.call-update) | async-done | bytes 14680080 | tf_op jit(solution)/shard_map/all_gather | solution.py:13
  330.2 0.0 copy-done
  330.2 12.5 %fusion.2 = f32[296,1792]{1,0:T(8,128)} fusion(bf16[1,296,1792]{2,1,0:T(8,128)(2,1)} %param.8, bf16[1,296,1792]{2,1,0:T(8,128)(2,1)} %param.7, bf16[296,4096]{1,0:T(8,128)(2,1)S(1)} %copy-done, bf16[4096,1792]{1,0:T(8,128)(2,1)} %all-gather.5.cloned.1.call-done), kind=kOutput, calls=%fused_computation.3 | convolution fusion | flops 4351664128 | bytes 21348352 | tf_op jit(solution)/shard_map/dot_general | solution.py:14
  342.7 3.2 copy.6
  345.9 0.0 copy-start.1
  345.9 0.0 reduce-scatter.10.cloned.1.call-update
  345.9 0.0 reduce-scatter.12.cloned.1.call-start
  346.0 38.9 %reduce-scatter.10.cloned.1.call-done = f32[448,296]{1,0:T(8,128)} async-done(((f32[1792,296]{1,0:T(8,128)}), f32[448,296]{1,0:T(8,128)}) %reduce-scatter.10.cloned.1.call-update) | async-done | bytes 530448
  384.9 0.0 reduce-scatter.12.cloned.1.call-update
  384.9 0.0 reduce-scatter.14.cloned.1.call-start
  384.9 26.8 %reduce-scatter.12.cloned.1.call-done = f32[224,296]{1,0:T(8,128)} async-done(((f32[448,296]{1,0:T(8,128)}), f32[224,296]{1,0:T(8,128)}) %reduce-scatter.12.cloned.1.call-update) | async-done | bytes 265232
  411.7 0.0 reduce-scatter.14.cloned.1.call-update
  411.7 20.6 %reduce-scatter.14.cloned.1.call-done = f32[112,296]{1,0:T(8,128)} async-done(((f32[224,296]{1,0:T(8,128)}), f32[112,296]{1,0:T(8,128)}) %reduce-scatter.14.cloned.1.call-update) | async-done | bytes 132624
  432.3 1.0 copy.11
  433.3 0.0 copy-done.1
  433.4 0.7 multiply_add_fusion
Async XLA Ops:
  6.5 323.6 %copy-start = (bf16[296,4096]{1,0:T(8,128)(2,1)S(1)}, bf16[296,4096]{1,0:T(8,128)(2,1)}, u32[]{:S(2)}) copy-start(bf16[296,4096]{1,0:T(8,128)(2,1)} %param.5) | copy-start | bytes 7274500
  6.5 60.4 %all-gather.3.cloned.1.call-start = ((), (), s32[]{:S(2)}) async-start(), calls=%async_computation.3 | async-start | bytes 4128768 | tf_op jit(solution)/shard_map/all_gather | solution.py:12
  7.3 322.9 %all-gather.5.cloned.1.call-start = ((), (), s32[]{:S(2)}) async-start(), calls=%async_computation.4 | async-start | bytes 18350080 | tf_op jit(solution)/shard_map/all_gather | solution.py:13
  66.9 317.9 %reduce-scatter.10.cloned.1.call-start = ((), (), s32[]{:S(2)}) async-start(), calls=%async_computation.5 | async-start | bytes 3440640
  345.9 87.5 %copy-start.1 = (bf16[296,112]{1,0:T(8,128)(2,1)S(1)}, bf16[296,112]{1,0:T(8,128)(2,1)}, u32[]{:S(2)}) copy-start(bf16[296,112]{1,0:T(8,128)(2,1)} %param.9) | copy-start | bytes 198916
  345.9 65.8 %reduce-scatter.12.cloned.1.call-start = ((), (), s32[]{:S(2)}) async-start(), calls=%async_computation.6 | async-start | bytes 1032192
  384.9 47.4 %reduce-scatter.14.cloned.1.call-start = ((), (), s32[]{:S(2)}) async-start(), calls=%async_computation.7 | async-start | bytes 516096
Sparse Core Ops, SparseCore 0:
  9.4 57.4 all-gather.2
  69.0 261.1 all-gather.4
  346.0 38.7 reduce-scatter.9
  387.5 24.1 reduce-scatter.11
  414.3 17.9 reduce-scatter.13
where the time goes:
time: 441 us
  waiting for transfers between devices  410 us (93%)
  between operations  13.2 us (3%)
  matrix products  12.5 us (3%)
    all_gather x1, waiting for transfers between devices, shards(): gathered = lax.all_gather(gathered, 'fz', axis=0, tiled=True)  263 us
    unnamed x8, waiting for transfers between devices  87.1 us
    all_gather x1, waiting for transfers between devices, shards(): gathered = lax.all_gather(cotangent, 'fy', axis=0, tiled=True)  59.6 us
    dot_general x1, matrix products, shards(): jnp.dot(hidden, gathered, preferred_element_type=jnp.float32)  12.5 us
  transfers between devices with their start and end apart: 5, of which 5 were waited for; matrix products, arithmetic and copies ran while one was open for 0% of the time, Pallas kernels for 0%

commit v1 on v0

--- a/solution.py
+++ b/solution.py
@@ -9,7 +9,10 @@
 
 
 def shards(hidden, cotangent, first_moment, second_moment, outer_momentum):
-    gathered = lax.all_gather(cotangent, "fy", axis=0, tiled=True)
+    count = lax.axis_size("fy")
+    pieces = jnp.stack([cotangent for _ in range(count)])
+    pieces = lax.all_to_all(pieces, "fy", split_axis=0, concat_axis=0)
+    gathered = jnp.concatenate(pieces, axis=0)
     gathered = lax.all_gather(gathered, "fz", axis=0, tiled=True)
     gradient = jnp.dot(hidden, gathered, preferred_element_type=jnp.float32) / gathered.shape[0]
     first_new = 0.9 * first_moment[0].astype(jnp.float32) + 0.1 * gradient

time: 441 us -> 474 us (1.075)
  blocking collectives: 0 us -> 89.5 us
  waiting for transfers between devices: 410 us -> 352 us
    all_to_all x0 -> x1, blocking collectives: none -> 89.5 us  [shards(): pieces = lax.all_to_all(pieces, 'fy', split_axis=0, concat_axis=0)]
    all_gather x1 -> x0, waiting for transfers between devices: 59.6 us -> none  [shards(): gathered = lax.all_gather(cotangent, 'fy', axis=0, tiled=True)]
    unnamed x8 -> x7, waiting for transfers between devices: 87.1 us -> 87.1 us
  transfers between devices with their start and end apart: 5 -> 4, of which waited for: 5 -> 4; matrix products, arithmetic and copies ran while one was open for 0% -> 0% of each run, Pallas kernels for 0% -> 0%
where the time goes in v1:
time: 474 us; the launch traced here: 473 us
  waiting for transfers between devices  352 us (74%)
  blocking collectives  89.5 us (19%)
  between operations  13.2 us (3%)
  matrix products  12.5 us (3%)
  local copies, waits for them, and re-layouts  5.65 us (1%)
    all_gather x1, waiting for transfers between devices, shards(): gathered = lax.all_gather(gathered, 'fz', axis=0, tiled=True)  265 us
    all_to_all x1, blocking collectives, shards(): pieces = lax.all_to_all(pieces, 'fy', split_axis=0, concat_axis=0)  89.5 us
    unnamed x7, waiting for transfers between devices  87.1 us
    dot_general x1, matrix products, shards(): jnp.dot(hidden, gathered, preferred_element_type=jnp.float32)  12.5 us
  transfers between devices with their start and end apart: 4, of which 4 were waited for; matrix products, arithmetic and copies ran while one was open for 0% of the time, Pallas kernels for 0%

profile of v1, /device:TPU:1, one launch (start us, length us, event | category | flops | bytes accessed | tf_op | source)
XLA Modules:
  0.0 473.4 jit_solution(2690406624657570414)
XLA Ops:
  6.5 0.0 copy-start
  6.5 0.0 all-gather.2.cloned.1.call-start
  6.5 1.4 stack.2
  8.0 89.5 %all_to_all.5 = bf16[8,128,1792]{2,1,0:T(8,128)(2,1)} all-to-all(bf16[8,128,1792]{2,1,0:T(8,128)(2,1)S(1)} %stack.2), channel_id=1, replica_groups=mesh['wx'=4,'wz'=2,'wc'=2,'fz'=4,'fy'=8] {'fy'}, dimensions={0} | all-to-all | bytes 7340032 | tf_op jit(solution)/shard_map/all_to_all | solution.py:14
  97.4 0.0 all-gather.2.cloned.1.call-update
  97.4 0.0 reduce-scatter.10.cloned.1.call-start
  97.5 264.7 %all-gather.2.cloned.1.call-done = bf16[4096,1792]{1,0:T(8,128)(2,1)} async-done(((bf16[1024,1792]{1,0:T(8,128)(2,1)}), bf16[4096,1792]{1,0:T(8,128)(2,1)}) %all-gather.2.cloned.1.call-update) | async-done | bytes 14680080 | tf_op jit(solution)/shard_map/all_gather | solution.py:16
  362.2 0.0 copy-done
  362.2 12.5 %fusion.2 = f32[296,1792]{1,0:T(8,128)} fusion(bf16[1,296,1792]{2,1,0:T(8,128)(2,1)} %param.8, bf16[1,296,1792]{2,1,0:T(8,128)(2,1)} %param.7, bf16[296,4096]{1,0:T(8,128)(2,1)S(1)} %copy-done, bf16[4096,1792]{1,0:T(8,128)(2,1)} %all-gather.2.cloned.1.call-done), kind=kOutput, calls=%fused_computation.3 | convolution fusion | flops 4351664128 | bytes 21348352 | tf_op jit(solution)/shard_map/dot_general | solution.py:17
  374.7 3.2 copy.6
  377.9 0.0 copy-start.1
  377.9 0.0 reduce-scatter.10.cloned.1.call-update
  377.9 0.0 reduce-scatter.12.cloned.1.call-start
  378.0 39.5 %reduce-scatter.10.cloned.1.call-done = f32[448,296]{1,0:T(8,128)} async-done(((f32[1792,296]{1,0:T(8,128)}), f32[448,296]{1,0:T(8,128)}) %reduce-scatter.10.cloned.1.call-update) | async-done | bytes 530448
  417.5 0.0 reduce-scatter.12.cloned.1.call-update
  417.5 0.0 reduce-scatter.14.cloned.1.call-start
  417.6 26.9 %reduce-scatter.12.cloned.1.call-done = f32[224,296]{1,0:T(8,128)} async-done(((f32[448,296]{1,0:T(8,128)}), f32[224,296]{1,0:T(8,128)}) %reduce-scatter.12.cloned.1.call-update) | async-done | bytes 265232
  444.5 0.0 reduce-scatter.14.cloned.1.call-update
  444.5 20.6 %reduce-scatter.14.cloned.1.call-done = f32[112,296]{1,0:T(8,128)} async-done(((f32[224,296]{1,0:T(8,128)}), f32[112,296]{1,0:T(8,128)}) %reduce-scatter.14.cloned.1.call-update) | async-done | bytes 132624
  465.1 1.0 copy.11
  466.1 0.0 copy-done.1
  466.1 0.7 multiply_add_fusion
Async XLA Ops:
  6.5 355.7 %copy-start = (bf16[296,4096]{1,0:T(8,128)(2,1)S(1)}, bf16[296,4096]{1,0:T(8,128)(2,1)}, u32[]{:S(2)}) copy-start(bf16[296,4096]{1,0:T(8,128)(2,1)} %param.5) | copy-start | bytes 7274500
  6.5 355.7 %all-gather.2.cloned.1.call-start = ((), (), s32[]{:S(2)}) async-start(), calls=%async_computation.4 | async-start | bytes 18350080 | tf_op jit(solution)/shard_map/all_gather | solution.py:16
  97.4 320.1 %reduce-scatter.10.cloned.1.call-start = ((), (), s32[]{:S(2)}) async-start(), calls=%async_computation.5 | async-start | bytes 3440640
  377.9 88.2 %copy-start.1 = (bf16[296,112]{1,0:T(8,128)(2,1)S(1)}, bf16[296,112]{1,0:T(8,128)(2,1)}, u32[]{:S(2)}) copy-start(bf16[296,112]{1,0:T(8,128)(2,1)} %param.9) | copy-start | bytes 198916
  377.9 66.5 %reduce-scatter.12.cloned.1.call-start = ((), (), s32[]{:S(2)}) async-start(), calls=%async_computation.6 | async-start | bytes 1032192
  417.5 47.6 %reduce-scatter.14.cloned.1.call-start = ((), (), s32[]{:S(2)}) async-start(), calls=%async_computation.7 | async-start | bytes 516096
Sparse Core Ops, SparseCore 0:
  97.6 264.5 all-gather.1
  378.1 39.3 reduce-scatter.9
  420.3 24.1 reduce-scatter.11
  447.1 17.9 reduce-scatter.13
